TPU v7x, 32 devices: a whole 2x2x4 slice. The times are simulated.
32 devices in a mesh: groups: 2 (over y), tm: 4 (over z), height: 2 (over x), chan: 2 (over core).
Axes of the slice: x: 2, y: 2, z: 4, core: 2. Of those that a mesh axis runs over, the one named last changes fastest.
Arguments:
- video: bfloat16 [16, 72, 320, 128], P(('groups', 'tm'), 'height', 'chan'), parts along dimension 0, may hold values from -52 to 52
- norm1_gain: float32 [320], P('chan'), may hold values from 0.25 to 1.75
- norm1_bias: float32 [320], P('chan'), may hold values from -3 to 3
- spatial_weight: bfloat16 [3, 3, 320, 320], P(None, None, 'tm', 'chan'), may hold values from -0.3125 to 0.3125
- spatial_bias: float32 [320], P('chan'), may hold values from -3 to 3
- norm2_gain: float32 [320], P('chan'), may hold values from 0.25 to 1.75
- norm2_bias: float32 [320], P('chan'), may hold values from -3 to 3
- temporal_weight: bfloat16 [3, 320, 320], P(None, 'tm', 'chan'), may hold values from -0.3125 to 0.3125
- temporal_bias: float32 [320], P('chan'), may hold values from -3 to 3
Outputs:
- clip_out: bfloat16 [16, 72, 320, 128], P(('groups', 'tm'), 'height', 'chan'), parts along dimension 0
There are 2 independent parts, one for each index of `groups`. A program takes and returns all parts, laid end to end along the dimension named above; an argument that names none is the same for every part. Nothing has to cross between parts.
All inputs are finite; a program needn't handle non-finite values.
Results may differ from a plain program's by a relative error of at most 0.0052.
Values may be sent and summed in bfloat16 or wider, within the bound.
No kernel may reach another device: no remote copies, remote signals or barrier semaphores. Data moves between devices by JAX's collectives and lax.ppermute only.
A program may use at most 128 MiB of HBM per device.

v0:
```python
import jax
import jax.numpy as jnp
from jax import lax
from jax.sharding import PartitionSpec as P

C = 320
GROUPS = 32
EPSILON = 1e-06


def with_halo(block, sides, width):
    for axis, dim in sides:
        count = lax.axis_size(axis)
        forward = [(i, i + 1) for i in range(count - 1)]
        backward = [(target, source) for source, target in forward]
        low = lax.ppermute(
            lax.slice_in_dim(block, block.shape[dim] - width, None, axis=dim), axis, forward
        )
        high = lax.ppermute(lax.slice_in_dim(block, 0, width, axis=dim), axis, backward)
        block = jnp.concatenate([low, block, high], axis=dim)
    return block


def spatial_taps(running, channel_slab, weight_piece, rows, width):
    for row_tap in range(3):
        for col_tap in range(3):
            window = channel_slab[:, row_tap : row_tap + rows, :, col_tap : col_tap + width]
            running = running + jnp.einsum(
                "frcw,co->frow",
                window,
                weight_piece[row_tap, col_tap],
                preferred_element_type=jnp.float32,
            )
    return running


def temporal_taps(running, channel_slab, weight_piece, frames):
    for frame_tap in range(3):
        window = channel_slab[frame_tap : frame_tap + frames]
        running = running + jnp.einsum(
            "frcw,co->frow", window, weight_piece[frame_tap], preferred_element_type=jnp.float32
        )
    return running


def body(
    video,
    norm1_gain,
    norm1_bias,
    spatial_weight,
    spatial_bias,
    norm2_gain,
    norm2_bias,
    temporal_weight,
    temporal_bias,
):
    frames, rows, local_chan, width = video.shape
    group_size = C // GROUPS
    local_groups = local_chan // group_size
    values = video.astype(jnp.float32)
    grouped = values.reshape(frames, rows, local_groups, group_size, width)
    entries = rows * lax.axis_size("height") * width * group_size
    totals = lax.psum(jnp.sum(grouped, axis=(1, 3, 4)), "height")
    average = (totals / entries).reshape(frames, 1, local_groups, 1, 1)
    centred = grouped - average
    squares = lax.psum(jnp.sum(centred * centred, axis=(1, 3, 4)), "height")
    variance = (squares / entries).reshape(frames, 1, local_groups, 1, 1)
    scaled = (centred * lax.rsqrt(variance + EPSILON)).reshape(frames, rows, local_chan, width)
    act_one = jax.nn.silu(scaled * norm1_gain[:, None] + norm1_bias[:, None]).astype(jnp.bfloat16)
    with_rows = with_halo(act_one, (("height", 1),), 1)
    all_inputs = lax.all_gather(with_rows, "chan", axis=2, tiled=True)
    padded = jnp.pad(all_inputs, ((0, 0), (0, 0), (0, 0), (1, 1)))
    empty = jnp.zeros((frames, rows, local_chan, width), jnp.float32)
    full_spatial = lax.all_gather(spatial_weight, "tm", axis=2, tiled=True)
    spatial_sum = spatial_taps(empty, padded, full_spatial, rows, width)
    hidden = (values + spatial_sum + spatial_bias[:, None]).astype(jnp.bfloat16)
    grouped_two = hidden.astype(jnp.float32).reshape(frames, rows, local_groups, group_size, width)
    entries_two = frames * lax.axis_size("tm") * entries
    totals_two = lax.psum(jnp.sum(grouped_two, axis=(0, 1, 3, 4)), ("tm", "height"))
    average_two = (totals_two / entries_two).reshape(1, 1, local_groups, 1, 1)
    centred_two = grouped_two - average_two
    squares_two = lax.psum(jnp.sum(centred_two * centred_two, axis=(0, 1, 3, 4)), ("tm", "height"))
    variance_two = (squares_two / entries_two).reshape(1, 1, local_groups, 1, 1)
    scaled_two = (centred_two * lax.rsqrt(variance_two + EPSILON)).reshape(
        frames, rows, local_chan, width
    )
    act_two = jax.nn.silu(scaled_two * norm2_gain[:, None] + norm2_bias[:, None]).astype(
        jnp.bfloat16
    )
    wide_two = lax.all_gather(act_two, "chan", axis=2, tiled=True)
    with_frames = with_halo(wide_two, (("tm", 0),), 1)
    full_temporal = lax.all_gather(temporal_weight, "tm", axis=1, tiled=True)
    temporal_sum = temporal_taps(empty, with_frames, full_temporal, frames)
    return (hidden.astype(jnp.float32) + temporal_sum + temporal_bias[:, None]).astype(jnp.bfloat16)


def solution(mesh):
    return jax.shard_map(
        body,
        mesh=mesh,
        in_specs=(
            P(("groups", "tm"), "height", "chan", None),
            P("chan"),
            P("chan"),
            P(None, None, "tm", "chan"),
            P("chan"),
            P("chan"),
            P("chan"),
            P(None, "tm", "chan"),
            P("chan"),
        ),
        out_specs=P(("groups", "tm"), "height", "chan", None),
        check_vma=False,
    )
```

profile of v0, /device:TPU:0, one launch (start us, length us, event | category | flops | bytes accessed | tf_op | source)
XLA Modules:
  0.0 309.7 jit_solution(8180734178120804956)
XLA Ops:
  6.5 2.5 convert_reduce_fusion.1
  9.2 5.8 %psum.28 = f32[2,16]{1,0:T(2,128)S(1)} all-reduce(f32[2,16]{1,0:T(2,128)S(1)} %reduce_sum.51), channel_id=1, replica_groups=mesh['groups'=2,'tm'=4,'height'=2,'chan'=2] {'height'}, use_global_device_ids=true, to_apply=%region_2.0 | all-reduce | flops 32 | bytes 256 | tf_op jit(solution)/shard_map/psum | solution.py:63
  15.2 2.7 fusion.13
  18.1 4.9 %psum.29 = f32[2,16]{1,0:T(2,128)S(1)} all-reduce(f32[2,16]{1,0:T(2,128)S(1)} %reduce_sum.54), channel_id=1, replica_groups=mesh['groups'=2,'tm'=4,'height'=2,'chan'=2] {'height'}, use_global_device_ids=true, to_apply=%region_5.6 | all-reduce | flops 32 | bytes 256 | tf_op jit(solution)/shard_map/psum | solution.py:66
  23.2 2.3 fusion.21
  25.6 4.1 %collective-permute-start = (bf16[2,1,160,128]{3,2,1,0:T(8,128)(2,1)S(1)}, bf16[2,1,160,128]{3,2,1,0:T(8,128)(2,1)S(1)}, u32[]{:S(2)}, u32[]{:S(2)}) collective-permute-start(bf16[2,1,160,128]{3,2,1,0:T(8,128)(2,1)S(1)} %get-tuple-element.7), channel_id=1, source_target_pairs={{0,2},{1,3},{4,6},{5,7},{8,10},{9,11},{12,14},{13,15},{16,18},{17,... | collective-permute-start | bytes 245768 | tf_op jit(solution)/shard_map/ppermute | solution.py:16
  29.7 1.3 collective-permute-start.1
  31.7 4.3 %collective-permute-done.1 = bf16[2,1,160,128]{3,2,1,0:T(8,128)(2,1)S(1)} collective-permute-done((bf16[2,1,160,128]{3,2,1,0:T(8,128)(2,1)S(1)}, bf16[2,1,160,128]{3,2,1,0:T(8,128)(2,1)S(1)}, u32[]{:S(2)}, u32[]{:S(2)}) %collective-permute-start.1) | collective-permute-done | bytes 81952 | tf_op jit(solution)/shard_map/ppermute | solution.py:19
  36.0 2.1 pad_maximum_fusion.4
  38.5 33.1 %all_gather.13 = bf16[3,3,320,160]{3,1,0,2:T(4,128)(2,1)S(1)} all-gather(bf16[3,3,80,160]{3,1,0,2:T(4,128)(2,1)S(1)} %copy.28), channel_id=1, replica_groups=mesh['groups'=2,'tm'=4,'height'=2,'chan'=2] {'tm'}, dimensions={2}, use_global_device_ids=true | all-gather | bytes 1152000 | tf_op jit(solution)/shard_map/all_gather | solution.py:74
  71.5 2.6 fusion.67
  77.8 4.6 %fusion.26 = f32[2,36,128,160]{2,3,1,0:T(8,128)S(1)} fusion(bf16[2,38,320,128]{3,2,1,0:T(8,128)(2,1)} %all-gather.3.cloned.1.call-done, bf16[1,1,320,160]{2,3,1,0:T(8,128)(2,1)S(1)} %copy.54), kind=kOutput, calls=%fused_computation.38 | convolution fusion | flops 943718400 | bytes 12226560 | tf_op jit(solution)/shard_map/frcw,co->frow/dot_general | solution.py:28
  82.5 4.3 %fusion.27 = f32[2,36,128,160]{2,3,1,0:T(8,128)} fusion(bf16[2,38,320,128]{3,2,1,0:T(8,128)(2,1)S(1)} %copy-done, bf16[1,1,320,160]{2,3,1,0:T(8,128)(2,1)S(1)} %copy.56), kind=kOutput, calls=%fused_computation.39 | convolution fusion | flops 943718400 | bytes 12226560 | tf_op jit(solution)/shard_map/frcw,co->frow/dot_general | solution.py:28
  86.8 4.4 %fusion.28 = f32[2,36,128,160]{2,3,1,0:T(8,128)} fusion(bf16[2,38,320,128]{3,2,1,0:T(8,128)(2,1)S(1)} %copy-done, bf16[1,1,320,160]{2,3,1,0:T(8,128)(2,1)S(1)} %copy.57), kind=kOutput, calls=%fused_computation.40 | convolution fusion | flops 943718400 | bytes 12226560 | tf_op jit(solution)/shard_map/frcw,co->frow/dot_general | solution.py:28
  91.2 4.3 %fusion.29 = f32[2,36,128,160]{2,3,1,0:T(8,128)} fusion(bf16[2,38,320,128]{3,2,1,0:T(8,128)(2,1)S(1)} %copy-done, bf16[1,1,320,160]{2,3,1,0:T(8,128)(2,1)S(1)} %copy.59), kind=kOutput, calls=%fused_computation.41 | convolution fusion | flops 943718400 | bytes 12226560 | tf_op jit(solution)/shard_map/frcw,co->frow/dot_general | solution.py:28
  95.5 4.4 %fusion.30 = f32[2,36,128,160]{2,3,1,0:T(8,128)} fusion(bf16[2,38,320,128]{3,2,1,0:T(8,128)(2,1)S(1)} %copy-done, bf16[1,1,320,160]{2,3,1,0:T(8,128)(2,1)S(1)} %copy.60), kind=kOutput, calls=%fused_computation.42 | convolution fusion | flops 943718400 | bytes 12226560 | tf_op jit(solution)/shard_map/frcw,co->frow/dot_general | solution.py:28
  100.0 4.2 %fusion.36 = f32[2,36,128,160]{2,3,1,0:T(8,128)} fusion(bf16[2,38,320,128]{3,2,1,0:T(8,128)(2,1)S(1)} %copy-done, bf16[1,1,320,160]{2,3,1,0:T(8,128)(2,1)S(1)} %copy-done.3), kind=kOutput, calls=%fused_computation.50 | convolution fusion | flops 943718400 | bytes 11919360 | tf_op jit(solution)/shard_map/frcw,co->frow/dot_general | solution.py:28
  104.2 4.4 %fusion.38 = f32[2,36,128,160]{2,3,1,0:T(8,128)} fusion(bf16[2,38,320,128]{3,2,1,0:T(8,128)(2,1)S(1)} %copy-done, bf16[1,1,320,160]{2,3,1,0:T(8,128)(2,1)S(1)} %copy-done.4), kind=kOutput, calls=%fused_computation.52 | convolution fusion | flops 943718400 | bytes 11919360 | tf_op jit(solution)/shard_map/frcw,co->frow/dot_general | solution.py:28
  108.6 4.2 %fusion.40 = f32[2,36,128,160]{2,3,1,0:T(8,128)} fusion(bf16[2,38,320,128]{3,2,1,0:T(8,128)(2,1)S(1)} %copy-done, bf16[1,1,320,160]{2,3,1,0:T(8,128)(2,1)S(1)} %copy-done.5), kind=kOutput, calls=%fused_computation.54 | convolution fusion | flops 943718400 | bytes 11919360 | tf_op jit(solution)/shard_map/frcw,co->frow/dot_general | solution.py:28
  112.8 17.5 %convert_reduce_fusion = (f32[160]{0:T(256)S(1)}, bf16[2,36,160,128]{3,2,1,0:T(8,128)(2,1)}) fusion(f32[160]{0:T(256)S(1)} %copy-done.8, bf16[2,38,320,128]{3,2,1,0:T(8,128)(2,1)S(1)} %copy-done, bf16[1,1,320,160]{2,3,1,0:T(8,128)(2,1)S(1)} %copy.62, f32[2,36,128,160]{2,3,1,0:T(8,128)} %fusion.36, f32[2,36,128,160]{2,3,1,0:T(8,128)} %fusion.30, ...), kind=kOutput, calls=%fused_computation.8 | convolution fusion | flops 964362112 | bytes 59413760 | tf_op jit(solution)/shard_map/frcw,co->frow/dot_general | solution.py:28
  130.5 19.8 %psum.30 = f32[16]{0:T(128)S(1)} all-reduce(f32[16]{0:T(128)S(1)} %reduce_sum.72), channel_id=1, replica_groups=mesh['groups'=2,'tm'=4,'height'=2,'chan'=2] {'tm','height'}, use_global_device_ids=true, to_apply=%region_8.9 | all-reduce | flops 16 | bytes 128 | tf_op jit(solution)/shard_map/psum | solution.py:79
  150.5 2.8 fusion.4
  153.4 17.1 %psum.31 = f32[16]{0:T(128)S(1)} all-reduce(f32[16]{0:T(128)S(1)} %reduce_sum.75), channel_id=1, replica_groups=mesh['groups'=2,'tm'=4,'height'=2,'chan'=2] {'tm','height'}, use_global_device_ids=true, to_apply=%region_11.12 | all-reduce | flops 16 | bytes 128 | tf_op jit(solution)/shard_map/psum | solution.py:82
  170.8 5.1 %fusion.12 = bf16[2,36,160,128]{3,2,1,0:T(8,128)(2,1)} fusion(bf16[2,36,160,128]{3,2,1,0:T(8,128)(2,1)} %get-tuple-element.22, f32[160]{0:T(256)S(1)} %copy-done.12, f32[160]{0:T(256)S(1)} %copy-done.13, f32[160]{0:T(256)S(1)} %mul.67, f32[160]{0:T(256)S(1)} %sub.33), kind=kLoop, calls=%fused_computation.24 | loop fusion | flops 14745600 | bytes 5900800 | tf_op jit(solution)/shard_map/convert_element_type | solution.py:87
  175.9 15.1 %all-gather.5.cloned.1.call-done = bf16[2,36,320,128]{3,2,1,0:T(8,128)(2,1)} async-done(((bf16[2,36,160,128]{3,2,1,0:T(8,128)(2,1)}), bf16[2,36,320,128]{3,2,1,0:T(8,128)(2,1)}) %all-gather.5.cloned.1.call-update) | async-done | bytes 5898256 | tf_op jit(solution)/shard_map/all_gather | solution.py:90
  190.9 5.6 %fusion.65 = (bf16[1,36,320,128]{3,2,1,0:T(8,128)(2,1)}, bf16[1,36,320,128]{3,2,1,0:T(8,128)(2,1)}) fusion(bf16[2,36,320,128]{3,2,1,0:T(8,128)(2,1)} %all-gather.5.cloned.1.call-done), kind=kLoop, calls=%fused_computation.82 | loop fusion | bytes 11796480 | tf_op jit(solution)/shard_map/slice | solution.py:19
  196.5 5.3 %collective-permute-start.2 = (bf16[1,36,320,128]{3,2,1,0:T(8,128)(2,1)}, bf16[1,36,320,128]{3,2,1,0:T(8,128)(2,1)}, u32[]{:S(2)}, u32[]{:S(2)}) collective-permute-start(bf16[1,36,320,128]{3,2,1,0:T(8,128)(2,1)} %get-tuple-element.6), channel_id=1, source_target_pairs={{0,4},{4,8},{8,12},{1,5},{5,9},{9,13},{2,6},{6,10},{10,14},{3,7},{... | collective-permute-start | bytes 8847368 | tf_op jit(solution)/shard_map/ppermute | solution.py:16
  201.9 1.3 collective-permute-start.3
  203.2 79.8 %all_gather.15 = bf16[3,320,160]{2,0,1:T(4,128)(2,1)S(1)} all-gather(bf16[3,80,160]{2,0,1:T(4,128)(2,1)S(1)} %copy.38), channel_id=1, replica_groups=mesh['groups'=2,'tm'=4,'height'=2,'chan'=2] {'tm'}, dimensions={1}, use_global_device_ids=true | all-gather | bytes 384000 | tf_op jit(solution)/shard_map/all_gather | solution.py:92
  284.3 4.5 %fusion.45 = f32[2,36,128,160]{2,3,1,0:T(8,128)S(1)} fusion(bf16[2,36,320,128]{3,2,1,0:T(8,128)(2,1)} %all-gather.5.cloned.1.call-done, bf16[1,320,160]{1,2,0:T(8,128)(2,1)S(1)} %copy.64), kind=kOutput, calls=%fused_computation.58 | convolution fusion | flops 943718400 | bytes 11898880 | tf_op jit(solution)/shard_map/frcw,co->frow/dot_general | solution.py:40
  288.9 6.2 %fusion.34 = f32[2,36,128,160]{2,3,1,0:T(8,128)} fusion(bf16[2,36,320,128]{3,2,1,0:T(8,128)(2,1)S(1)} %bitcast.94, bf16[1,36,320,128]{3,2,1,0:T(8,128)(2,1)} %collective-permute-done.2, bf16[1,320,160]{1,2,0:T(8,128)(2,1)S(1)} %copy.63), kind=kOutput, calls=%fused_computation.48 | convolution fusion | flops 955514880 | bytes 14848000 | tf_op jit(solution)/shard_map/frcw,co->frow/dot_general | solution.py:40
  295.1 7.7 %fusion.25 = bf16[2,36,160,128]{3,2,1,0:T(8,128)(2,1)} fusion(bf16[2,36,160,128]{3,2,1,0:T(8,128)(2,1)S(1)} %copy-done.1, f32[2,36,128,160]{2,3,1,0:T(8,128)} %fusion.34, f32[2,36,128,160]{2,3,1,0:T(8,128)S(1)} %fusion.45, f32[160]{0:T(256)S(1)} %copy-done.9, bf16[1,36,320,128]{3,2,1,0:T(8,128)(2,1)} %collective-permute-done.3, ...), kind=kOutput, calls=%fused_computation.37 | convolution fusion | flops 964362240 | bytes 26645120 | tf_op jit(solution)/shard_map/frcw,co->frow/dot_general | solution.py:40
  (77 shorter events, 7.6 us)
Async XLA Ops:
  6.5 16.7 %copy-start.2 = (bf16[2,36,160,128]{3,2,1,0:T(8,128)(2,1)S(1)}, bf16[2,36,160,128]{3,2,1,0:T(8,128)(2,1)}, u32[]{:S(2)}) copy-start(bf16[2,36,160,128]{3,2,1,0:T(8,128)(2,1)} %param.9) | copy-start | bytes 8847364
  6.5 16.7 %copy-start.11 = (f32[160]{0:T(256)S(1)}, f32[160]{0:T(256)}, u32[]{:S(2)}) copy-start(f32[160]{0:T(256)} %param.10) | copy-start | bytes 1924
  6.5 16.7 %copy-start.10 = (f32[160]{0:T(256)S(1)}, f32[160]{0:T(256)}, u32[]{:S(2)}) copy-start(f32[160]{0:T(256)} %param.11) | copy-start | bytes 1924
  6.5 71.3 %all-gather.3.cloned.1.call-start = ((), (), s32[]{:S(2)}) async-start(), calls=%async_computation | async-start | bytes 9338880 | tf_op jit(solution)/shard_map/all_gather | solution.py:71
  25.6 12.6 %copy-start.6 = (bf16[3,3,80,160]{3,2,1,0:T(8,128)(2,1)S(1)}, bf16[3,3,80,160]{3,2,1,0:T(8,128)(2,1)}, u32[]{:S(2)}) copy-start(bf16[3,3,80,160]{3,2,1,0:T(8,128)(2,1)} %param.12) | copy-start | bytes 691204
  25.6 6.1 %collective-permute-start = (bf16[2,1,160,128]{3,2,1,0:T(8,128)(2,1)S(1)}, bf16[2,1,160,128]{3,2,1,0:T(8,128)(2,1)S(1)}, u32[]{:S(2)}, u32[]{:S(2)}) collective-permute-start(bf16[2,1,160,128]{3,2,1,0:T(8,128)(2,1)S(1)} %get-tuple-element.7), channel_id=1, source_target_pairs={{0,2},{1,3},{4,6},{5,7},{8,10},{9,11},{12,14},{13,15},{16,18},{17,... | collective-permute-start | bytes 245768 | tf_op jit(solution)/shard_map/ppermute | solution.py:16
  29.7 6.3 %collective-permute-start.1 = (bf16[2,1,160,128]{3,2,1,0:T(8,128)(2,1)S(1)}, bf16[2,1,160,128]{3,2,1,0:T(8,128)(2,1)S(1)}, u32[]{:S(2)}, u32[]{:S(2)}) collective-permute-start(bf16[2,1,160,128]{3,2,1,0:T(8,128)(2,1)S(1)} %get-tuple-element.8), channel_id=1, source_target_pairs={{2,0},{3,1},{6,4},{7,5},{10,8},{11,9},{14,12},{15,13},{18,16},{19,... | collective-permute-start | bytes 245768 | tf_op jit(solution)/shard_map/ppermute | solution.py:19
  38.1 152.8 %all-gather.5.cloned.1.call-start = ((), (), s32[]{:S(2)}) async-start(), calls=%async_computation.1 | async-start | bytes 8847360 | tf_op jit(solution)/shard_map/all_gather | solution.py:90
  77.8 4.7 %copy-start = (bf16[2,38,320,128]{3,2,1,0:T(8,128)(2,1)S(1)}, bf16[2,38,320,128]{3,2,1,0:T(8,128)(2,1)}, u32[]{:S(2)}) copy-start(bf16[2,38,320,128]{3,2,1,0:T(8,128)(2,1)} %all-gather.3.cloned.1.call-done) | copy-start | bytes 18677764
  95.5 4.4 %copy-start.3 = (bf16[1,1,320,160]{2,3,1,0:T(8,128)(2,1)S(1)}, bf16[1,1,320,160]{2,3,1,0:T(8,128)(2,1)}, u32[]{:S(2)}) copy-start(bf16[1,1,320,160]{2,3,1,0:T(8,128)(2,1)} %copy.61) | copy-start | bytes 307204
  100.0 4.2 %copy-start.4 = (bf16[1,1,320,160]{2,3,1,0:T(8,128)(2,1)S(1)}, bf16[1,1,320,160]{2,3,1,0:T(8,128)(2,1)}, u32[]{:S(2)}) copy-start(bf16[1,1,320,160]{2,3,1,0:T(8,128)(2,1)} %copy.58) | copy-start | bytes 307204
  104.2 4.4 %copy-start.5 = (bf16[1,1,320,160]{2,3,1,0:T(8,128)(2,1)S(1)}, bf16[1,1,320,160]{2,3,1,0:T(8,128)(2,1)}, u32[]{:S(2)}) copy-start(bf16[1,1,320,160]{2,3,1,0:T(8,128)(2,1)} %copy.55) | copy-start | bytes 307204
  108.6 4.2 %copy-start.8 = (f32[160]{0:T(256)S(1)}, f32[160]{0:T(256)}, u32[]{:S(2)}) copy-start(f32[160]{0:T(256)} %param.13) | copy-start | bytes 1924
  112.8 57.9 %copy-start.12 = (f32[160]{0:T(256)S(1)}, f32[160]{0:T(256)}, u32[]{:S(2)}) copy-start(f32[160]{0:T(256)} %param.15) | copy-start | bytes 1924
  112.8 58.0 %copy-start.13 = (f32[160]{0:T(256)S(1)}, f32[160]{0:T(256)}, u32[]{:S(2)}) copy-start(f32[160]{0:T(256)} %param.14) | copy-start | bytes 1924
  175.9 27.3 %copy-start.7 = (bf16[3,80,160]{2,1,0:T(8,128)(2,1)S(1)}, bf16[3,80,160]{2,1,0:T(8,128)(2,1)}, u32[]{:S(2)}) copy-start(bf16[3,80,160]{2,1,0:T(8,128)(2,1)} %param.16) | copy-start | bytes 230404
  196.5 92.3 %collective-permute-start.2 = (bf16[1,36,320,128]{3,2,1,0:T(8,128)(2,1)}, bf16[1,36,320,128]{3,2,1,0:T(8,128)(2,1)}, u32[]{:S(2)}, u32[]{:S(2)}) collective-permute-start(bf16[1,36,320,128]{3,2,1,0:T(8,128)(2,1)} %get-tuple-element.6), channel_id=1, source_target_pairs={{0,4},{4,8},{8,12},{1,5},{5,9},{9,13},{2,6},{6,10},{10,14},{3,7},{... | collective-permute-start | bytes 8847368 | tf_op jit(solution)/shard_map/ppermute | solution.py:16
  201.9 93.3 %collective-permute-start.3 = (bf16[1,36,320,128]{3,2,1,0:T(8,128)(2,1)}, bf16[1,36,320,128]{3,2,1,0:T(8,128)(2,1)}, u32[]{:S(2)}, u32[]{:S(2)}) collective-permute-start(bf16[1,36,320,128]{3,2,1,0:T(8,128)(2,1)} %get-tuple-element.5), channel_id=1, source_target_pairs={{4,0},{8,4},{12,8},{5,1},{9,5},{13,9},{6,2},{10,6},{14,10},{7,3},{... | collective-permute-start | bytes 8847368 | tf_op jit(solution)/shard_map/ppermute | solution.py:19
  284.1 4.8 %slice-start = ((s8[5898240]{0:T(1024)(128)(4,1)}), s8[1703936]{0:T(1024)(128)(4,1)S(1)}, s32[]{:S(2)}) async-start(s8[5898240]{0:T(1024)(128)(4,1)} %bitcast.93), calls=%async_computation.2 | async-start | bytes 3407872
  284.3 4.6 %slice-start.1 = ((s8[5898240]{0:T(1024)(128)(4,1)}), s8[4194304]{0:T(1024)(128)(4,1)S(1)}, s32[]{:S(2)}) async-start(s8[5898240]{0:T(1024)(128)(4,1)} %bitcast.93), calls=%async_computation.3 | async-start | bytes 8388608
  288.8 6.3 %copy-start.1 = (bf16[2,36,160,128]{3,2,1,0:T(8,128)(2,1)S(1)}, bf16[2,36,160,128]{3,2,1,0:T(8,128)(2,1)}, u32[]{:S(2)}) copy-start(bf16[2,36,160,128]{3,2,1,0:T(8,128)(2,1)} %get-tuple-element.22) | copy-start | bytes 8847364
  288.9 6.3 %copy-start.9 = (f32[160]{0:T(256)S(1)}, f32[160]{0:T(256)}, u32[]{:S(2)}) copy-start(f32[160]{0:T(256)} %param.17) | copy-start | bytes 1924
Sparse Core Ops, SparseCore 0:
  38.3 16.9 all-gather.2
  176.0 14.9 all-gather.4
where the time goes:
time: 310 us
  blocking collectives  161 us (52%)
  matrix products  70.9 us (23%)
  waiting for transfers between devices  20.2 us (7%)
  other arithmetic  17.9 us (6%)
  local copies, waits for them, and re-layouts  14.5 us (5%)
  between operations  13.7 us (4%)
  starting transfers between devices  12 us (4%)
    all_gather x1, blocking collectives, body(): full_temporal = lax.all_gather(temporal_weight, 'tm', axis=1, tiled=True)  79.8 us
    dot_general x9, matrix products, spatial_taps(): jnp.einsum('frcw,co->frow', window, weight_piece[row_tap, col_tap], prefe...  52.5 us
    all_gather x1, blocking collectives, body(): full_spatial = lax.all_gather(spatial_weight, 'tm', axis=2, tiled=True)  33.1 us
    psum x1, blocking collectives, body(): lax.psum(jnp.sum(grouped_two, axis=(0, 1, 3, 4)), ('tm', 'height'))  19.8 us
    dot_general x3, matrix products, temporal_taps(): jnp.einsum('frcw,co->frow', window, weight_piece[frame_tap], preferred_el...  18.4 us
    psum x1, blocking collectives, body(): lax.psum(jnp.sum(centred_two * centred_two, axis=(0, 1, 3, 4)), ('tm', 'h...  17.1 us
    all_gather x1, waiting for transfers between devices, body(): wide_two = lax.all_gather(act_two, 'chan', axis=2, tiled=True)  15.1 us
    ppermute x2, starting transfers between devices, with_halo(): lax.ppermute(lax.slice_in_dim(block, block.shape[dim] - width, None, axis...  9.4 us
  transfers between devices with their start and end apart: 6, of which 3 were waited for; matrix products, arithmetic and copies ran while one was open for 6% of the time, Pallas kernels for 0%

commit v1 on v0

--- a/solution.py
+++ b/solution.py
@@ -79,7 +79,10 @@
     totals_two = lax.psum(jnp.sum(grouped_two, axis=(0, 1, 3, 4)), ("tm", "height"))
     average_two = (totals_two / entries_two).reshape(1, 1, local_groups, 1, 1)
     centred_two = grouped_two - average_two
-    squares_two = lax.psum(jnp.sum(centred_two * centred_two, axis=(0, 1, 3, 4)), ("tm", "height"))
+    squares_two = jnp.sum(
+        lax.all_gather(jnp.sum(centred_two * centred_two, axis=(0, 1, 3, 4)), ("tm", "height")),
+        axis=0,
+    )
     variance_two = (squares_two / entries_two).reshape(1, 1, local_groups, 1, 1)
     scaled_two = (centred_two * lax.rsqrt(variance_two + EPSILON)).reshape(
         frames, rows, local_chan, width

time: 310 us -> 312 us (level)
    psum x1 -> x0, blocking collectives: 17.1 us -> none  [body(): lax.psum(jnp.sum(centred_two * centred_two, axis=(0, 1, 3, 4)), ('tm', 'h...]
    unnamed x0 -> x1, blocking collectives: none -> 17.1 us
where the time goes in v1:
time: 312 us; the launch traced here: 311 us
  blocking collectives  160 us (51%)
  matrix products  70.9 us (23%)
  waiting for transfers between devices  20.1 us (6%)
  other arithmetic  17.9 us (6%)
  local copies, waits for them, and re-layouts  15.5 us (5%)
  between operations  14.4 us (5%)
  starting transfers between devices  12 us (4%)
    all_gather x1, blocking collectives, body(): full_temporal = lax.all_gather(temporal_weight, 'tm', axis=1, tiled=True)  79.8 us
    dot_general x9, matrix products, spatial_taps(): jnp.einsum('frcw,co->frow', window, weight_piece[row_tap, col_tap], prefe...  52.4 us
    all_gather x1, blocking collectives, body(): full_spatial = lax.all_gather(spatial_weight, 'tm', axis=2, tiled=True)  33.1 us
    psum x1, blocking collectives, body(): lax.psum(jnp.sum(grouped_two, axis=(0, 1, 3, 4)), ('tm', 'height'))  19.8 us
    dot_general x3, matrix products, temporal_taps(): jnp.einsum('frcw,co->frow', window, weight_piece[frame_tap], preferred_el...  18.4 us
    unnamed x1, blocking collectives  17.1 us
    all_gather x1, waiting for transfers between devices, body(): wide_two = lax.all_gather(act_two, 'chan', axis=2, tiled=True)  15.1 us
    ppermute x2, starting transfers between devices, with_halo(): lax.ppermute(lax.slice_in_dim(block, block.shape[dim] - width, None, axis...  9.4 us
  transfers between devices with their start and end apart: 6, of which 3 were waited for; matrix products, arithmetic and copies ran while one was open for 6% of the time, Pallas kernels for 0%

profile of v1, /device:TPU:0, one launch (start us, length us, event | category | flops | bytes accessed | tf_op | source)
XLA Modules:
  0.0 311.4 jit_solution(11176957732759495957)
XLA Ops:
  6.5 2.5 convert_reduce_fusion.1
  9.2 5.8 %psum.21 = f32[2,16]{1,0:T(2,128)S(1)} all-reduce(f32[2,16]{1,0:T(2,128)S(1)} %reduce_sum.59), channel_id=1, replica_groups=mesh['groups'=2,'tm'=4,'height'=2,'chan'=2] {'height'}, use_global_device_ids=true, to_apply=%region_2.0 | all-reduce | flops 32 | bytes 256 | tf_op jit(solution)/shard_map/psum | solution.py:63
  15.2 2.7 fusion.13
  18.1 4.9 %psum.22 = f32[2,16]{1,0:T(2,128)S(1)} all-reduce(f32[2,16]{1,0:T(2,128)S(1)} %reduce_sum.62), channel_id=1, replica_groups=mesh['groups'=2,'tm'=4,'height'=2,'chan'=2] {'height'}, use_global_device_ids=true, to_apply=%region_5.6 | all-reduce | flops 32 | bytes 256 | tf_op jit(solution)/shard_map/psum | solution.py:66
  23.2 2.3 fusion.21
  25.6 4.1 %collective-permute-start = (bf16[2,1,160,128]{3,2,1,0:T(8,128)(2,1)S(1)}, bf16[2,1,160,128]{3,2,1,0:T(8,128)(2,1)S(1)}, u32[]{:S(2)}, u32[]{:S(2)}) collective-permute-start(bf16[2,1,160,128]{3,2,1,0:T(8,128)(2,1)S(1)} %get-tuple-element.7), channel_id=1, source_target_pairs={{0,2},{1,3},{4,6},{5,7},{8,10},{9,11},{12,14},{13,15},{16,18},{17,... | collective-permute-start | bytes 245768 | tf_op jit(solution)/shard_map/ppermute | solution.py:16
  29.7 1.3 collective-permute-start.1
  31.7 4.3 %collective-permute-done.1 = bf16[2,1,160,128]{3,2,1,0:T(8,128)(2,1)S(1)} collective-permute-done((bf16[2,1,160,128]{3,2,1,0:T(8,128)(2,1)S(1)}, bf16[2,1,160,128]{3,2,1,0:T(8,128)(2,1)S(1)}, u32[]{:S(2)}, u32[]{:S(2)}) %collective-permute-start.1) | collective-permute-done | bytes 81952 | tf_op jit(solution)/shard_map/ppermute | solution.py:19
  36.0 2.1 pad_maximum_fusion.4
  38.5 33.1 %all_gather.19 = bf16[3,3,320,160]{3,1,0,2:T(4,128)(2,1)S(1)} all-gather(bf16[3,3,80,160]{3,1,0,2:T(4,128)(2,1)S(1)} %copy.28), channel_id=1, replica_groups=mesh['groups'=2,'tm'=4,'height'=2,'chan'=2] {'tm'}, dimensions={2}, use_global_device_ids=true | all-gather | bytes 1152000 | tf_op jit(solution)/shard_map/all_gather | solution.py:74
  71.6 2.6 fusion.67
  78.5 4.6 %fusion.26 = f32[2,36,128,160]{2,3,1,0:T(8,128)S(1)} fusion(bf16[2,38,320,128]{3,2,1,0:T(8,128)(2,1)} %all-gather.4.cloned.1.call-done, bf16[1,1,320,160]{2,3,1,0:T(8,128)(2,1)S(1)} %copy.54), kind=kOutput, calls=%fused_computation.38 | convolution fusion | flops 943718400 | bytes 12226560 | tf_op jit(solution)/shard_map/frcw,co->frow/dot_general | solution.py:28
  83.1 4.3 %fusion.27 = f32[2,36,128,160]{2,3,1,0:T(8,128)} fusion(bf16[2,38,320,128]{3,2,1,0:T(8,128)(2,1)S(1)} %copy-done, bf16[1,1,320,160]{2,3,1,0:T(8,128)(2,1)S(1)} %copy.56), kind=kOutput, calls=%fused_computation.39 | convolution fusion | flops 943718400 | bytes 12226560 | tf_op jit(solution)/shard_map/frcw,co->frow/dot_general | solution.py:28
  87.5 4.4 %fusion.28 = f32[2,36,128,160]{2,3,1,0:T(8,128)} fusion(bf16[2,38,320,128]{3,2,1,0:T(8,128)(2,1)S(1)} %copy-done, bf16[1,1,320,160]{2,3,1,0:T(8,128)(2,1)S(1)} %copy.57), kind=kOutput, calls=%fused_computation.40 | convolution fusion | flops 943718400 | bytes 12226560 | tf_op jit(solution)/shard_map/frcw,co->frow/dot_general | solution.py:28
  91.8 4.3 %fusion.29 = f32[2,36,128,160]{2,3,1,0:T(8,128)} fusion(bf16[2,38,320,128]{3,2,1,0:T(8,128)(2,1)S(1)} %copy-done, bf16[1,1,320,160]{2,3,1,0:T(8,128)(2,1)S(1)} %copy.59), kind=kOutput, calls=%fused_computation.41 | convolution fusion | flops 943718400 | bytes 12226560 | tf_op jit(solution)/shard_map/frcw,co->frow/dot_general | solution.py:28
  96.2 4.4 %fusion.30 = f32[2,36,128,160]{2,3,1,0:T(8,128)} fusion(bf16[2,38,320,128]{3,2,1,0:T(8,128)(2,1)S(1)} %copy-done, bf16[1,1,320,160]{2,3,1,0:T(8,128)(2,1)S(1)} %copy.60), kind=kOutput, calls=%fused_computation.42 | convolution fusion | flops 943718400 | bytes 12226560 | tf_op jit(solution)/shard_map/frcw,co->frow/dot_general | solution.py:28
  100.6 4.2 %fusion.36 = f32[2,36,128,160]{2,3,1,0:T(8,128)} fusion(bf16[2,38,320,128]{3,2,1,0:T(8,128)(2,1)S(1)} %copy-done, bf16[1,1,320,160]{2,3,1,0:T(8,128)(2,1)S(1)} %copy-done.3), kind=kOutput, calls=%fused_computation.50 | convolution fusion | flops 943718400 | bytes 11919360 | tf_op jit(solution)/shard_map/frcw,co->frow/dot_general | solution.py:28
  104.8 4.4 %fusion.38 = f32[2,36,128,160]{2,3,1,0:T(8,128)} fusion(bf16[2,38,320,128]{3,2,1,0:T(8,128)(2,1)S(1)} %copy-done, bf16[1,1,320,160]{2,3,1,0:T(8,128)(2,1)S(1)} %copy-done.4), kind=kOutput, calls=%fused_computation.52 | convolution fusion | flops 943718400 | bytes 11919360 | tf_op jit(solution)/shard_map/frcw,co->frow/dot_general | solution.py:28
  109.3 4.2 %fusion.40 = f32[2,36,128,160]{2,3,1,0:T(8,128)} fusion(bf16[2,38,320,128]{3,2,1,0:T(8,128)(2,1)S(1)} %copy-done, bf16[1,1,320,160]{2,3,1,0:T(8,128)(2,1)S(1)} %copy-done.5), kind=kOutput, calls=%fused_computation.54 | convolution fusion | flops 943718400 | bytes 11919360 | tf_op jit(solution)/shard_map/frcw,co->frow/dot_general | solution.py:28
  113.5 17.5 %convert_reduce_fusion = (f32[160]{0:T(256)S(1)}, bf16[2,36,160,128]{3,2,1,0:T(8,128)(2,1)}) fusion(f32[160]{0:T(256)S(1)} %copy-done.8, bf16[2,38,320,128]{3,2,1,0:T(8,128)(2,1)S(1)} %copy-done, bf16[1,1,320,160]{2,3,1,0:T(8,128)(2,1)S(1)} %copy.62, f32[2,36,128,160]{2,3,1,0:T(8,128)} %fusion.36, f32[2,36,128,160]{2,3,1,0:T(8,128)} %fusion.30, ...), kind=kOutput, calls=%fused_computation.8 | convolution fusion | flops 964362112 | bytes 59413760 | tf_op jit(solution)/shard_map/frcw,co->frow/dot_general | solution.py:28
  131.9 19.8 %psum.23 = f32[16]{0:T(128)S(1)} all-reduce(f32[16]{0:T(128)S(1)} %reduce_sum.81), channel_id=1, replica_groups=mesh['groups'=2,'tm'=4,'height'=2,'chan'=2] {'tm','height'}, use_global_device_ids=true, to_apply=%region_8.9 | all-reduce | flops 16 | bytes 128 | tf_op jit(solution)/shard_map/psum | solution.py:79
  151.8 2.8 fusion.4
  155.1 17.1 %all-reduce.1 = f32[128]{0:T(128)S(1)} all-reduce(f32[128]{0:T(128)S(1)} %dynamic-update-slice), channel_id=2, replica_groups=mesh['groups'=2,'tm'=4,'height'=2,'chan'=2] {'tm','height'}, use_global_device_ids=true, to_apply=%add.1 | all-reduce | flops 128 | bytes 1024
  172.5 5.1 %fusion.12 = bf16[2,36,160,128]{3,2,1,0:T(8,128)(2,1)} fusion(bf16[2,36,160,128]{3,2,1,0:T(8,128)(2,1)} %get-tuple-element.22, f32[160]{0:T(256)S(1)} %copy-done.12, f32[160]{0:T(256)S(1)} %copy-done.13, f32[160]{0:T(256)S(1)} %mul.67, f32[160]{0:T(256)S(1)} %sub.33), kind=kLoop, calls=%fused_computation.24 | loop fusion | flops 14745600 | bytes 5900800 | tf_op jit(solution)/shard_map/convert_element_type | solution.py:90
  177.6 15.1 %all-gather.6.cloned.1.call-done = bf16[2,36,320,128]{3,2,1,0:T(8,128)(2,1)} async-done(((bf16[2,36,160,128]{3,2,1,0:T(8,128)(2,1)}), bf16[2,36,320,128]{3,2,1,0:T(8,128)(2,1)}) %all-gather.6.cloned.1.call-update) | async-done | bytes 5898256 | tf_op jit(solution)/shard_map/all_gather | solution.py:93
  192.6 5.6 %fusion.65 = (bf16[1,36,320,128]{3,2,1,0:T(8,128)(2,1)}, bf16[1,36,320,128]{3,2,1,0:T(8,128)(2,1)}) fusion(bf16[2,36,320,128]{3,2,1,0:T(8,128)(2,1)} %all-gather.6.cloned.1.call-done), kind=kLoop, calls=%fused_computation.82 | loop fusion | bytes 11796480 | tf_op jit(solution)/shard_map/slice | solution.py:19
  198.2 5.3 %collective-permute-start.2 = (bf16[1,36,320,128]{3,2,1,0:T(8,128)(2,1)}, bf16[1,36,320,128]{3,2,1,0:T(8,128)(2,1)}, u32[]{:S(2)}, u32[]{:S(2)}) collective-permute-start(bf16[1,36,320,128]{3,2,1,0:T(8,128)(2,1)} %get-tuple-element.6), channel_id=1, source_target_pairs={{0,4},{4,8},{8,12},{1,5},{5,9},{9,13},{2,6},{6,10},{10,14},{3,7},{... | collective-permute-start | bytes 8847368 | tf_op jit(solution)/shard_map/ppermute | solution.py:16
  203.5 1.3 collective-permute-start.3
  204.9 79.8 %all_gather.23 = bf16[3,320,160]{2,0,1:T(4,128)(2,1)S(1)} all-gather(bf16[3,80,160]{2,0,1:T(4,128)(2,1)S(1)} %copy.38), channel_id=1, replica_groups=mesh['groups'=2,'tm'=4,'height'=2,'chan'=2] {'tm'}, dimensions={1}, use_global_device_ids=true | all-gather | bytes 384000 | tf_op jit(solution)/shard_map/all_gather | solution.py:95
  286.0 4.5 %fusion.45 = f32[2,36,128,160]{2,3,1,0:T(8,128)S(1)} fusion(bf16[2,36,320,128]{3,2,1,0:T(8,128)(2,1)} %all-gather.6.cloned.1.call-done, bf16[1,320,160]{1,2,0:T(8,128)(2,1)S(1)} %copy.64), kind=kOutput, calls=%fused_computation.58 | convolution fusion | flops 943718400 | bytes 11898880 | tf_op jit(solution)/shard_map/frcw,co->frow/dot_general | solution.py:40
  290.6 6.2 %fusion.34 = f32[2,36,128,160]{2,3,1,0:T(8,128)} fusion(bf16[2,36,320,128]{3,2,1,0:T(8,128)(2,1)S(1)} %bitcast.95, bf16[1,36,320,128]{3,2,1,0:T(8,128)(2,1)} %collective-permute-done.2, bf16[1,320,160]{1,2,0:T(8,128)(2,1)S(1)} %copy.63), kind=kOutput, calls=%fused_computation.48 | convolution fusion | flops 955514880 | bytes 14848000 | tf_op jit(solution)/shard_map/frcw,co->frow/dot_general | solution.py:40
  296.8 7.7 %fusion.25 = bf16[2,36,160,128]{3,2,1,0:T(8,128)(2,1)} fusion(bf16[2,36,160,128]{3,2,1,0:T(8,128)(2,1)S(1)} %copy-done.1, f32[2,36,128,160]{2,3,1,0:T(8,128)} %fusion.34, f32[2,36,128,160]{2,3,1,0:T(8,128)S(1)} %fusion.45, f32[160]{0:T(256)S(1)} %copy-done.9, bf16[1,36,320,128]{3,2,1,0:T(8,128)(2,1)} %collective-permute-done.3, ...), kind=kOutput, calls=%fused_computation.37 | convolution fusion | flops 964362240 | bytes 26645120 | tf_op jit(solution)/shard_map/frcw,co->frow/dot_general | solution.py:40
  (84 shorter events, 8.6 us)
Async XLA Ops:
  6.5 16.7 %copy-start.2 = (bf16[2,36,160,128]{3,2,1,0:T(8,128)(2,1)S(1)}, bf16[2,36,160,128]{3,2,1,0:T(8,128)(2,1)}, u32[]{:S(2)}) copy-start(bf16[2,36,160,128]{3,2,1,0:T(8,128)(2,1)} %param.9) | copy-start | bytes 8847364
  6.5 16.7 %copy-start.11 = (f32[160]{0:T(256)S(1)}, f32[160]{0:T(256)}, u32[]{:S(2)}) copy-start(f32[160]{0:T(256)} %param.10) | copy-start | bytes 1924
  6.5 16.7 %copy-start.10 = (f32[160]{0:T(256)S(1)}, f32[160]{0:T(256)}, u32[]{:S(2)}) copy-start(f32[160]{0:T(256)} %param.11) | copy-start | bytes 1924
  6.5 72.0 %all-gather.4.cloned.1.call-start = ((), (), s32[]{:S(2)}) async-start(), calls=%async_computation | async-start | bytes 9338880 | tf_op jit(solution)/shard_map/all_gather | solution.py:71
  25.6 12.6 %copy-start.6 = (bf16[3,3,80,160]{3,2,1,0:T(8,128)(2,1)S(1)}, bf16[3,3,80,160]{3,2,1,0:T(8,128)(2,1)}, u32[]{:S(2)}) copy-start(bf16[3,3,80,160]{3,2,1,0:T(8,128)(2,1)} %param.12) | copy-start | bytes 691204
  25.6 6.1 %collective-permute-start = (bf16[2,1,160,128]{3,2,1,0:T(8,128)(2,1)S(1)}, bf16[2,1,160,128]{3,2,1,0:T(8,128)(2,1)S(1)}, u32[]{:S(2)}, u32[]{:S(2)}) collective-permute-start(bf16[2,1,160,128]{3,2,1,0:T(8,128)(2,1)S(1)} %get-tuple-element.7), channel_id=1, source_target_pairs={{0,2},{1,3},{4,6},{5,7},{8,10},{9,11},{12,14},{13,15},{16,18},{17,... | collective-permute-start | bytes 245768 | tf_op jit(solution)/shard_map/ppermute | solution.py:16
  29.7 6.3 %collective-permute-start.1 = (bf16[2,1,160,128]{3,2,1,0:T(8,128)(2,1)S(1)}, bf16[2,1,160,128]{3,2,1,0:T(8,128)(2,1)S(1)}, u32[]{:S(2)}, u32[]{:S(2)}) collective-permute-start(bf16[2,1,160,128]{3,2,1,0:T(8,128)(2,1)S(1)} %get-tuple-element.8), channel_id=1, source_target_pairs={{2,0},{3,1},{6,4},{7,5},{10,8},{11,9},{14,12},{15,13},{18,16},{19,... | collective-permute-start | bytes 245768 | tf_op jit(solution)/shard_map/ppermute | solution.py:19
  38.1 154.5 %all-gather.6.cloned.1.call-start = ((), (), s32[]{:S(2)}) async-start(), calls=%async_computation.1 | async-start | bytes 8847360 | tf_op jit(solution)/shard_map/all_gather | solution.py:93
  38.5 39.4 %copy-start.14 = (u32[32]{0:T(128)S(1)}, u32[32]{0:T(128)}, u32[]{:S(2)}) copy-start(u32[32]{0:T(128)} %constant.25) | copy-start | bytes 388
  78.5 4.6 %copy-start = (bf16[2,38,320,128]{3,2,1,0:T(8,128)(2,1)S(1)}, bf16[2,38,320,128]{3,2,1,0:T(8,128)(2,1)}, u32[]{:S(2)}) copy-start(bf16[2,38,320,128]{3,2,1,0:T(8,128)(2,1)} %all-gather.4.cloned.1.call-done) | copy-start | bytes 18677764
  96.2 4.4 %copy-start.3 = (bf16[1,1,320,160]{2,3,1,0:T(8,128)(2,1)S(1)}, bf16[1,1,320,160]{2,3,1,0:T(8,128)(2,1)}, u32[]{:S(2)}) copy-start(bf16[1,1,320,160]{2,3,1,0:T(8,128)(2,1)} %copy.61) | copy-start | bytes 307204
  100.6 4.2 %copy-start.4 = (bf16[1,1,320,160]{2,3,1,0:T(8,128)(2,1)S(1)}, bf16[1,1,320,160]{2,3,1,0:T(8,128)(2,1)}, u32[]{:S(2)}) copy-start(bf16[1,1,320,160]{2,3,1,0:T(8,128)(2,1)} %copy.58) | copy-start | bytes 307204
  104.8 4.4 %copy-start.5 = (bf16[1,1,320,160]{2,3,1,0:T(8,128)(2,1)S(1)}, bf16[1,1,320,160]{2,3,1,0:T(8,128)(2,1)}, u32[]{:S(2)}) copy-start(bf16[1,1,320,160]{2,3,1,0:T(8,128)(2,1)} %copy.55) | copy-start | bytes 307204
  109.3 4.2 %copy-start.8 = (f32[160]{0:T(256)S(1)}, f32[160]{0:T(256)}, u32[]{:S(2)}) copy-start(f32[160]{0:T(256)} %param.13) | copy-start | bytes 1924
  113.5 59.0 %copy-start.12 = (f32[160]{0:T(256)S(1)}, f32[160]{0:T(256)}, u32[]{:S(2)}) copy-start(f32[160]{0:T(256)} %param.15) | copy-start | bytes 1924
  113.5 59.0 %copy-start.13 = (f32[160]{0:T(256)S(1)}, f32[160]{0:T(256)}, u32[]{:S(2)}) copy-start(f32[160]{0:T(256)} %param.14) | copy-start | bytes 1924
  177.6 27.3 %copy-start.7 = (bf16[3,80,160]{2,1,0:T(8,128)(2,1)S(1)}, bf16[3,80,160]{2,1,0:T(8,128)(2,1)}, u32[]{:S(2)}) copy-start(bf16[3,80,160]{2,1,0:T(8,128)(2,1)} %param.16) | copy-start | bytes 230404
  198.2 92.3 %collective-permute-start.2 = (bf16[1,36,320,128]{3,2,1,0:T(8,128)(2,1)}, bf16[1,36,320,128]{3,2,1,0:T(8,128)(2,1)}, u32[]{:S(2)}, u32[]{:S(2)}) collective-permute-start(bf16[1,36,320,128]{3,2,1,0:T(8,128)(2,1)} %get-tuple-element.6), channel_id=1, source_target_pairs={{0,4},{4,8},{8,12},{1,5},{5,9},{9,13},{2,6},{6,10},{10,14},{3,7},{... | collective-permute-start | bytes 8847368 | tf_op jit(solution)/shard_map/ppermute | solution.py:16
  203.5 93.3 %collective-permute-start.3 = (bf16[1,36,320,128]{3,2,1,0:T(8,128)(2,1)}, bf16[1,36,320,128]{3,2,1,0:T(8,128)(2,1)}, u32[]{:S(2)}, u32[]{:S(2)}) collective-permute-start(bf16[1,36,320,128]{3,2,1,0:T(8,128)(2,1)} %get-tuple-element.5), channel_id=1, source_target_pairs={{4,0},{8,4},{12,8},{5,1},{9,5},{13,9},{6,2},{10,6},{14,10},{7,3},{... | collective-permute-start | bytes 8847368 | tf_op jit(solution)/shard_map/ppermute | solution.py:19
  285.8 4.8 %slice-start = ((s8[5898240]{0:T(1024)(128)(4,1)}), s8[1703936]{0:T(1024)(128)(4,1)S(1)}, s32[]{:S(2)}) async-start(s8[5898240]{0:T(1024)(128)(4,1)} %bitcast.94), calls=%async_computation.2 | async-start | bytes 3407872
  286.0 4.6 %slice-start.1 = ((s8[5898240]{0:T(1024)(128)(4,1)}), s8[4194304]{0:T(1024)(128)(4,1)S(1)}, s32[]{:S(2)}) async-start(s8[5898240]{0:T(1024)(128)(4,1)} %bitcast.94), calls=%async_computation.3 | async-start | bytes 8388608
  290.5 6.3 %copy-start.1 = (bf16[2,36,160,128]{3,2,1,0:T(8,128)(2,1)S(1)}, bf16[2,36,160,128]{3,2,1,0:T(8,128)(2,1)}, u32[]{:S(2)}) copy-start(bf16[2,36,160,128]{3,2,1,0:T(8,128)(2,1)} %get-tuple-element.22) | copy-start | bytes 8847364
  290.5 6.3 %copy-start.9 = (f32[160]{0:T(256)S(1)}, f32[160]{0:T(256)}, u32[]{:S(2)}) copy-start(f32[160]{0:T(256)} %param.17) | copy-start | bytes 1924
Sparse Core Ops, SparseCore 0:
  38.3 16.9 all-gather.3
  177.7 14.8 all-gather.5
